TPU v7x, 256 devices: a whole 4x4x8 slice. The times are simulated.
256 devices in a mesh: ctx: 16 (over z, x_hi), head: 16 (over x_lo, y, core).
Axes of the slice: x: 4 (x_hi: 2, x_lo: 2; x = x_hi * 2 + x_lo), y: 4, z: 8, core: 2. Of those that a mesh axis runs over, the one named last changes fastest.
Arguments:
- queries: bfloat16 [16384, 8192], P('ctx', 'head'), may hold values from -5.5 to 5.5
- keys: bfloat16 [16384, 512], P(('ctx', 'head')), may hold values from -5.5 to 5.5
- values: bfloat16 [16384, 512], P(('ctx', 'head')), may hold values from -6 to 6
- comp_k_weight: float32 [32, 512], replicated, may hold values from -0.79549513 to 0.79549513
- comp_v_weight: float32 [32, 512], replicated, may hold values from -1 to 1
- gate_logits: float32 [3, 64, 16384], P(None, 'head', 'ctx'), may hold values from -6 to 6
- sel_tiles: int32 [64, 64], replicated, may hold values from 0 to 243, as said below
Outputs:
- attended: bfloat16 [16384, 8192], P('ctx', 'head')
Inputs may be any that keep to these rules, and one draw needn't show every extreme that they name: `sel_tiles`: among the indices of the query blocks of one ctx shard (4 blocks) for one group, exactly 2 distinct tiles lie in each ctx shard up to and including their own and none in later ones; the first index of every query block names a tile among the first 4 tiles of its own ctx shard; indices may repeat within a block.
All inputs are finite; a program needn't handle non-finite values.
Results may differ from a plain program's by a relative error of at most 0.012.
Values may be sent and summed in bfloat16 or wider, within the bound.
No kernel may reach another device: no remote copies, remote signals or barrier semaphores. Data moves between devices by JAX's collectives and lax.ppermute only.
A program may use at most 64 MiB of HBM per device.

v0:
```python
import jax
import jax.numpy as jnp
from jax import lax
from jax.sharding import PartitionSpec as P

H = 64
G = 4
HD = 128
KERN = 32
STRIDE = 16
TILE = 64
TOPK = 16
WIN = 512
QB = 256
CAP = 2


def shifted(block, axis, distance):
    devices = range(lax.axis_size(axis))
    route = [(i - distance, i) for i in devices if i - distance in devices]
    return lax.ppermute(block, axis, route)


def online_step(folded, query_head, block_kv, allowed):
    running_max, running_sum, accum_out = folded
    scores = jnp.einsum(
        "qd,kd->qk", query_head, block_kv[:, :HD], preferred_element_type=jnp.float32
    ) * HD ** (-0.5)
    block_peak = jnp.max(jnp.where(allowed, scores, -jnp.inf), axis=-1)
    fresh_max = jnp.maximum(running_max, block_peak)
    weights = jnp.where(allowed, jnp.exp(scores - fresh_max[:, None]), 0.0)
    shrink = jnp.exp(running_max - fresh_max)
    running_sum = running_sum * shrink + jnp.sum(weights, axis=-1)
    product = jnp.dot(
        weights.astype(jnp.bfloat16), block_kv[:, HD:], preferred_element_type=jnp.float32
    )
    accum_out = accum_out * shrink[:, None] + product
    return (fresh_max, running_sum, accum_out)


def heads_step(folded, query_heads, block_kv, allowed):

    def per_head(element):
        return online_step((element[0], element[1], element[2]), element[3], block_kv, allowed)

    return lax.map(per_head, (folded[0], folded[1], folded[2], query_heads))


def finish(folded):
    return folded[2] / folded[1][..., None]


def local(queries, keys, values, comp_k_weight, comp_v_weight, gate_logits, sel_tiles):
    ctx_count = lax.axis_size("ctx")
    ctx_index = lax.axis_index("ctx")
    head_index = lax.axis_index("head")
    local_rows = queries.shape[0]
    local_heads = queries.shape[1] // HD
    group_index = head_index * local_heads // (H // G)
    all_keys, all_values = (
        lax.all_gather(keys, "head", axis=0, tiled=True),
        lax.all_gather(values, "head", axis=0, tiled=True),
    )
    group_keys = lax.dynamic_slice_in_dim(all_keys, group_index * HD, HD, 1)
    group_values = lax.dynamic_slice_in_dim(all_values, group_index * HD, HD, 1)
    group_kv = jnp.concatenate([group_keys, group_values], axis=1)
    positions = ctx_index * local_rows + jnp.arange(local_rows)
    query_heads = queries.reshape(local_rows, local_heads, HD).transpose(1, 0, 2)
    tail_rows = shifted(group_kv[: KERN - STRIDE], "ctx", -1)
    extended = jnp.concatenate([group_kv, tail_rows], axis=0)
    comp_weight = jnp.concatenate(
        [
            lax.dynamic_slice_in_dim(comp_k_weight, group_index * HD, HD, 1),
            lax.dynamic_slice_in_dim(comp_v_weight, group_index * HD, HD, 1),
        ],
        axis=1,
    )
    comp_local = local_rows // STRIDE
    first_half = extended[:local_rows].reshape(comp_local, STRIDE, 2 * HD).astype(jnp.float32)
    second_half = (
        extended[STRIDE : STRIDE + local_rows]
        .reshape(comp_local, STRIDE, 2 * HD)
        .astype(jnp.float32)
    )
    compressed = (
        jnp.sum(first_half * comp_weight[None, :STRIDE], 1)
        + jnp.sum(second_half * comp_weight[None, STRIDE:], 1)
    ).astype(jnp.bfloat16)
    sink_init = (
        jnp.zeros((local_heads, local_rows), jnp.float32),
        jnp.ones((local_heads, local_rows), jnp.float32),
        jnp.zeros((local_heads, local_rows, HD), jnp.float32),
    )
    shard_rows = lax.all_gather(compressed, "ctx", axis=0, tiled=True)
    row_count = shard_rows.shape[0]
    wide_block = min(row_count, 512)
    grouped = shard_rows.reshape(row_count // wide_block, wide_block, 2 * HD)

    def scan_step(running, element):
        block_kv, block_index = element
        block_end = (block_index * wide_block + jnp.arange(wide_block)) * STRIDE + KERN - 1
        allowed = block_end[None, :] <= positions[:, None]
        return (heads_step(running, query_heads, block_kv, allowed), None)

    result, unused = lax.scan(scan_step, sink_init, (grouped, jnp.arange(row_count // wide_block)))
    comp_out = finish(result)
    previous = shifted(group_kv[local_rows - WIN :], "ctx", 1)
    window_kv = jnp.concatenate([previous, group_kv], axis=0)

    def window_block(block_index):
        row_begin = block_index * WIN
        query_part = lax.dynamic_slice_in_dim(query_heads, row_begin, WIN, 1)
        kv_part = lax.dynamic_slice_in_dim(window_kv, row_begin, 2 * WIN, 0)
        key_pos = ctx_index * local_rows + row_begin - WIN + jnp.arange(2 * WIN)
        query_pos = ctx_index * local_rows + row_begin + jnp.arange(WIN)
        allowed = (
            (key_pos[None, :] <= query_pos[:, None])
            & (key_pos[None, :] > query_pos[:, None] - WIN)
            & (key_pos[None, :] >= 0)
        )
        window_init = (
            jnp.full((local_heads, WIN), -jnp.inf, jnp.float32),
            jnp.zeros((local_heads, WIN), jnp.float32),
            jnp.zeros((local_heads, WIN, HD), jnp.float32),
        )
        return finish(heads_step(window_init, query_part, kv_part, allowed))

    win_blocks = lax.map(window_block, jnp.arange(local_rows // WIN))
    win_out = win_blocks.transpose(1, 0, 2, 3).reshape(local_heads, local_rows, HD)
    block_count = local_rows // QB
    tiles_shard = local_rows // TILE
    group_tiles = lax.dynamic_slice_in_dim(sel_tiles, group_index * TOPK, TOPK, 1)
    own_tiles = lax.dynamic_slice_in_dim(group_tiles, ctx_index * block_count, block_count, 0)
    own_flat = own_tiles.reshape(-1)
    query_blocks = query_heads.reshape(local_heads, block_count, QB, HD).transpose(1, 0, 2, 3)
    sel_init = (
        jnp.zeros((block_count, local_heads, QB), jnp.float32),
        jnp.ones((block_count, local_heads, QB), jnp.float32),
        jnp.zeros((block_count, local_heads, QB, HD), jnp.float32),
    )
    requests = group_tiles.reshape(ctx_count, block_count * TOPK)
    local_ids = ctx_index * tiles_shard + jnp.arange(tiles_shard)
    present = jnp.any(requests[:, :, None] == local_ids[None, None, :], axis=1)
    order_rank = jnp.cumsum(present.astype(jnp.int32), axis=1) - 1
    picked = present[:, None, :] & (order_rank[:, None, :] == jnp.arange(CAP)[None, :, None])
    outbox = jnp.einsum(
        "dct,tx->dcx",
        picked.astype(jnp.bfloat16),
        group_kv.reshape(tiles_shard, TILE * 2 * HD),
        preferred_element_type=jnp.float32,
    ).astype(jnp.bfloat16)
    received = lax.all_to_all(outbox, "ctx", split_axis=0, concat_axis=0, tiled=True)
    all_ids = jnp.arange(ctx_count * tiles_shard).reshape(ctx_count, tiles_shard)
    wanted = jnp.any(own_flat[:, None, None] == all_ids[None, :, :], axis=0)
    wanted_rank = jnp.cumsum(wanted.astype(jnp.int32), axis=1) - 1
    chosen = wanted[:, None, :] & (wanted_rank[:, None, :] == jnp.arange(CAP)[None, :, None])
    slot_tile = jnp.sum(jnp.where(chosen, all_ids[:, None, :], 0), axis=2).reshape(-1)
    slot_ok = jnp.any(chosen, axis=2).reshape(-1)
    slot_kv = received.reshape(ctx_count * CAP * TILE, 2 * HD)
    key_pos = (slot_tile[:, None] * TILE + jnp.arange(TILE)[None, :]).reshape(-1)

    def per_block(element):
        block_max, block_sum, block_out, block_query, block_tiles, block_index = element
        is_named = slot_ok & jnp.any(block_tiles[:, None] == slot_tile[None, :], axis=0)
        key_ok = jnp.repeat(is_named, TILE)
        query_pos = ctx_index * local_rows + block_index * QB + jnp.arange(QB)
        allowed = key_ok[None, :] & (key_pos[None, :] <= query_pos[:, None])
        return heads_step((block_max, block_sum, block_out), block_query, slot_kv, allowed)

    sel_state = lax.map(
        per_block,
        (sel_init[0], sel_init[1], sel_init[2], query_blocks, own_tiles, jnp.arange(block_count)),
    )
    sel_out = finish(sel_state).transpose(1, 0, 2, 3).reshape(local_heads, local_rows, HD)
    gate_values = jax.nn.sigmoid(gate_logits)
    combined = (
        gate_values[0][..., None] * comp_out
        + gate_values[1][..., None] * sel_out
        + gate_values[2][..., None] * win_out
    )
    return combined.transpose(1, 0, 2).reshape(local_rows, local_heads * HD).astype(jnp.bfloat16)


def solution(mesh):
    placed = (
        P("ctx", "head"),
        P(("ctx", "head"), None),
        P(("ctx", "head"), None),
        P(),
        P(),
        P(None, "head", "ctx"),
        P(),
    )
    return jax.shard_map(
        local, mesh=mesh, in_specs=placed, out_specs=P("ctx", "head"), check_vma=False
    )
```

profile of v0, /device:TPU:6, one launch (start us, length us, event | category | flops | bytes accessed | tf_op | source)
XLA Modules:
  0.0 365.0 jit_solution(1468088390830321323)
XLA Ops:
  16.6 30.0 %all-gather.5.cloned.1.call-done = bf16[1024,512]{1,0:T(8,128)(2,1)} async-done(((bf16[64,512]{1,0:T(8,128)(2,1)}), bf16[1024,512]{1,0:T(8,128)(2,1)}) %all-gather.5.cloned.1.call-update) | async-done | bytes 1048592 | tf_op jit(solution)/shard_map/all_gather | solution.py:62
  47.7 35.7 %all-gather.3.cloned.1.call-done = bf16[1024,512]{1,0:T(8,128)(2,1)} async-done(((bf16[64,512]{1,0:T(8,128)(2,1)}), bf16[1024,512]{1,0:T(8,128)(2,1)}) %all-gather.3.cloned.1.call-update) | async-done | bytes 1048592 | tf_op jit(solution)/shard_map/all_gather | solution.py:61
  84.9 3.2 collective-permute-start
  89.2 2.1 copy.45
  91.2 10.0 %all-to-all-start = ((bf16[16,2,16384]{2,1,0:T(2,128)(2,1)}), bf16[16,2,16384]{2,1,0:T(2,128)(2,1)}, u32[]{:S(2)}, u32[]{:S(2)}) async-start(bf16[16,2,16384]{2,1,0:T(2,128)(2,1)} %copy.45), calls=%async_computation | async-start | bytes 2097152 | tf_op jit(solution)/shard_map/all_to_all | solution.py:152
  101.2 3.4 collective-permute-start.1
  104.9 60.8 %all_gather.11 = bf16[1024,256]{1,0:T(8,128)(2,1)S(1)} all-gather(bf16[64,256]{1,0:T(8,128)(2,1)S(1)} %add_convert_fusion), channel_id=1, replica_groups=mesh['ctx'=16,'head'=16] {'ctx'}, dimensions={0}, use_global_device_ids=true | all-gather | bytes 557056 | tf_op jit(solution)/shard_map/all_gather | solution.py:94
  167.1 40.8 %while.135 = (s32[]{:T(128)}, f32[4,1024]{1,0:T(4,128)S(1)}, f32[4,1024]{1,0:T(4,128)S(1)}, f32[4,1024,128]{2,1,0:T(8,128)}, bf16[2,512,256]{2,1,0:T(8,128)(2,1)...) while((s32[]{:T(128)}, f32[4,1024]{1,0:T(4,128)S(1)}, ...), condition=%wide.region_7.8_spmd.clone, body=%wide.region_2.7_spmd.clone.sunk | while | flops 276044288 | bytes 9548170 | solution.py:105
  168.5 19.0 %while.139 = (s32[]{:T(128)}, f32[4,1024]{1,0:T(4,128)S(1)}, f32[4,1024]{1,0:T(4,128)S(1)}, f32[4,1024,128]{2,1,0:T(8,128)}, bf16[4,1024,128]{2,1,0:T(8,128)(2,1...) while((s32[]{:T(128)}, f32[4,1024]{1,0:T(4,128)S(1)}, ...), condition=%wide.region_6.6_spmd.clone.clone, body=%wide.region_3.5_spmd.clone.clone.sunk | while | flops 276041728 | bytes 9017481 | solution.py:46
  188.9 19.0 %while.139 = (s32[]{:T(128)}, f32[4,1024]{1,0:T(4,128)S(1)}, f32[4,1024]{1,0:T(4,128)S(1)}, f32[4,1024,128]{2,1,0:T(8,128)}, bf16[4,1024,128]{2,1,0:T(8,128)(2,1...) while((s32[]{:T(128)}, f32[4,1024]{1,0:T(4,128)S(1)}, ...), condition=%wide.region_6.6_spmd.clone.clone, body=%wide.region_3.5_spmd.clone.clone.sunk | while | flops 276041728 | bytes 9017481 | solution.py:46
  209.0 49.2 %while.133 = (s32[]{:T(128)}, f32[2,4,512,128]{3,2,1,0:T(8,128)}, s32[2]{0:T(128)S(1)}, bf16[4,1024,128]{2,1,0:T(8,128)(2,1)}, bf16[1536,256]{1,0:T(8,128)(2,1)S...) while((s32[]{:T(128)}, f32[2,4,512,128]{3,2,1,0:T(8,128)}, ...), condition=%wide.region_26.27_spmd, body=%wide.region_21.26_spmd.sunk | while | flops 280826368 | bytes 17762856 | solution.py:128
  210.3 1.9 constant_dynamic-slice_fusion.14
  213.0 19.2 %while.138 = (s32[]{:T(128)}, f32[4,512]{1,0:T(4,128)S(1)}, f32[4,512,128]{2,1,0:T(8,128)S(1)}, bf16[4,512,128]{2,1,0:T(8,128)(2,1)}, bf16[1024,256]{1,0:T(8,128...) while((s32[]{:T(128)}, f32[4,512]{1,0:T(4,128)S(1)}, ...), condition=%wide.region_25.25_spmd.clone, body=%wide.region_22.24_spmd.clone.sunk | while | flops 280560128 | bytes 7259265 | solution.py:46
  213.0 1.8 select_reduce_fusion.6
  216.0 1.9 fusion.107
  217.8 1.8 select_reduce_fusion.6
  220.8 1.9 fusion.107
  222.7 1.8 select_reduce_fusion.6
  225.6 1.9 fusion.107
  227.5 1.9 select_reduce_fusion.6
  230.4 1.9 fusion.107
  234.8 1.9 constant_dynamic-slice_fusion.14
  237.6 19.2 %while.138 = (s32[]{:T(128)}, f32[4,512]{1,0:T(4,128)S(1)}, f32[4,512,128]{2,1,0:T(8,128)S(1)}, bf16[4,512,128]{2,1,0:T(8,128)(2,1)}, bf16[1024,256]{1,0:T(8,128...) while((s32[]{:T(128)}, f32[4,512]{1,0:T(4,128)S(1)}, ...), condition=%wide.region_25.25_spmd.clone, body=%wide.region_22.24_spmd.clone.sunk | while | flops 280560128 | bytes 7259265 | solution.py:46
  237.6 1.8 select_reduce_fusion.6
  240.5 1.9 fusion.107
  242.4 1.9 select_reduce_fusion.6
  245.4 1.9 fusion.107
  247.2 1.8 select_reduce_fusion.6
  250.2 1.9 fusion.107
  252.0 1.9 select_reduce_fusion.6
  255.0 1.9 fusion.107
  258.2 3.1 copy.52
  261.3 2.5 reshape.241
  263.9 86.8 %while.137 = (s32[]{:T(128)}, f32[4,4,256]{2,0,1:T(4,128)S(1)}, f32[4,4,256,128]{3,2,0,1:T(8,128)}, bf16[4,4,256,128]{3,2,0,1:T(8,128)(2,1)}, s32[4,16]{1,0:T(4,...) while((s32[]{:T(128)}, f32[4,4,256]{2,0,1:T(4,128)S(1)}, ...), condition=%wide.wide.region_20.21_spmd.clone, body=%wide.wide.region_14.20_spmd.clone.sunk | while | flops 276336640 | bytes 9205774 | solution.py:170
  267.2 17.5 %while.140 = (s32[]{:T(128)}, f32[4,256]{1,0:T(4,128)S(1)}, f32[4,256,128]{2,1,0:T(8,128)S(1)}, bf16[4,256,128]{2,1,0:T(8,128)(2,1)S(1)}, bf16[2048,256]{1,0:T(8...) while((s32[]{:T(128)}, f32[4,256]{1,0:T(4,128)S(1)}, ...), condition=%wide.region_19.19_spmd.clone, body=%wide.region_16.18_spmd.clone.sunk | while | flops 276333312 | bytes 7583865 | solution.py:46
  269.8 1.8 fusion.98
  274.1 1.8 fusion.98
  275.9 1.7 select_reduce_fusion.5
  278.5 1.8 fusion.98
  280.3 1.7 select_reduce_fusion.5
  282.9 1.8 fusion.98
  288.9 17.5 %while.140 = (s32[]{:T(128)}, f32[4,256]{1,0:T(4,128)S(1)}, f32[4,256,128]{2,1,0:T(8,128)S(1)}, bf16[4,256,128]{2,1,0:T(8,128)(2,1)S(1)}, bf16[2048,256]{1,0:T(8...) while((s32[]{:T(128)}, f32[4,256]{1,0:T(4,128)S(1)}, ...), condition=%wide.region_19.19_spmd.clone, body=%wide.region_16.18_spmd.clone.sunk | while | flops 276333312 | bytes 7583865 | solution.py:46
  291.4 1.8 fusion.98
  293.2 1.7 select_reduce_fusion.5
  295.8 1.8 fusion.98
  300.2 1.8 fusion.98
  302.0 1.7 select_reduce_fusion.5
  304.6 1.8 fusion.98
  310.5 17.5 %while.140 = (s32[]{:T(128)}, f32[4,256]{1,0:T(4,128)S(1)}, f32[4,256,128]{2,1,0:T(8,128)S(1)}, bf16[4,256,128]{2,1,0:T(8,128)(2,1)S(1)}, bf16[2048,256]{1,0:T(8...) while((s32[]{:T(128)}, f32[4,256]{1,0:T(4,128)S(1)}, ...), condition=%wide.region_19.19_spmd.clone, body=%wide.region_16.18_spmd.clone.sunk | while | flops 276333312 | bytes 7583865 | solution.py:46
  313.1 1.8 fusion.98
  314.9 1.7 select_reduce_fusion.5
  317.5 1.8 fusion.98
  319.3 1.7 select_reduce_fusion.5
  321.9 1.8 fusion.98
  323.7 1.7 select_reduce_fusion.5
  326.2 1.8 fusion.98
  332.2 17.5 %while.140 = (s32[]{:T(128)}, f32[4,256]{1,0:T(4,128)S(1)}, f32[4,256,128]{2,1,0:T(8,128)S(1)}, bf16[4,256,128]{2,1,0:T(8,128)(2,1)S(1)}, bf16[2048,256]{1,0:T(8...) while((s32[]{:T(128)}, f32[4,256]{1,0:T(4,128)S(1)}, ...), condition=%wide.region_19.19_spmd.clone, body=%wide.region_16.18_spmd.clone.sunk | while | flops 276333312 | bytes 7583865 | solution.py:46
  334.8 1.8 fusion.98
  339.2 1.8 fusion.98
  341.0 1.7 select_reduce_fusion.5
  343.5 1.8 fusion.98
  347.9 1.8 fusion.98
  350.7 2.1 broadcast_divide_fusion
  353.5 2.8 fusion.64
  (347 shorter events, 113.3 us)
Async XLA Ops:
  6.5 40.1 %all-gather.5.cloned.1.call-start = ((), (), s32[]{:S(2)}) async-start(), calls=%async_computation.2 | async-start | bytes 1114112 | tf_op jit(solution)/shard_map/all_gather | solution.py:62
  7.3 76.1 %all-gather.3.cloned.1.call-start = ((), (), s32[]{:S(2)}) async-start(), calls=%async_computation.1 | async-start | bytes 1114112 | tf_op jit(solution)/shard_map/all_gather | solution.py:61
  8.1 2.8 copy-start.10
  8.1 7.9 %copy-start.9 = (f32[3,4,1024]{2,1,0:T(4,128)S(1)}, f32[3,4,1024]{2,1,0:T(4,128)}, u32[]{:S(2)}) copy-start(f32[3,4,1024]{2,1,0:T(4,128)} %param.24) | copy-start | bytes 147460
  11.0 0.5 copy-start.14
  12.4 2.9 copy-start.11
  84.9 19.7 %collective-permute-start = (bf16[16,256]{1,0:T(8,128)(2,1)S(1)}, bf16[16,256]{1,0:T(8,128)(2,1)S(1)}, u32[]{:S(2)}, u32[]{:S(2)}) collective-permute-start(bf16[16,256]{1,0:T(8,128)(2,1)S(1)} %fusion.73), channel_id=1, source_target_pairs={{16,0},{32,16},{48,32},{64,48},{80,64},{96,80},{112,96},{128,112},... | collective-permute-start | bytes 24584 | tf_op jit(solution)/shard_map/ppermute | solution.py:21
  91.2 170.1 %all-to-all-start = ((bf16[16,2,16384]{2,1,0:T(2,128)(2,1)}), bf16[16,2,16384]{2,1,0:T(2,128)(2,1)}, u32[]{:S(2)}, u32[]{:S(2)}) async-start(bf16[16,2,16384]{2,1,0:T(2,128)(2,1)} %copy.45), calls=%async_computation | async-start | bytes 2097152 | tf_op jit(solution)/shard_map/all_to_all | solution.py:152
  101.2 106.7 %collective-permute-start.1 = (bf16[512,256]{1,0:T(8,128)(2,1)}, bf16[512,256]{1,0:T(8,128)(2,1)}, u32[]{:S(2)}, u32[]{:S(2)}) collective-permute-start(bf16[512,256]{1,0:T(8,128)(2,1)} %fusion.67), channel_id=1, source_target_pairs={{0,16},{16,32},{32,48},{48,64},{64,80},{80,96},{96,112},{112,128},... | collective-permute-start | bytes 786440 | tf_op jit(solution)/shard_map/ppermute | solution.py:21
  207.9 1.1 copy-start.4
  209.0 4.0 %copy-start.1 = (bf16[1536,256]{1,0:T(8,128)(2,1)}, bf16[1536,256]{1,0:T(8,128)(2,1)S(1)}, u32[]{:S(2)}) copy-start(bf16[1536,256]{1,0:T(8,128)(2,1)S(1)} %get-tuple-element.1592) | copy-start | bytes 2359300 | tf_op jit(solution)/shard_map/while
  232.3 1.4 copy-start.2
  233.6 4.0 %copy-start.1 = (bf16[1536,256]{1,0:T(8,128)(2,1)}, bf16[1536,256]{1,0:T(8,128)(2,1)S(1)}, u32[]{:S(2)}) copy-start(bf16[1536,256]{1,0:T(8,128)(2,1)S(1)} %get-tuple-element.1592) | copy-start | bytes 2359300 | tf_op jit(solution)/shard_map/while
  256.9 1.3 copy-start.2
  261.3 2.6 copy-start.12
  261.3 2.6 copy-start.13
  261.3 2.6 copy-start.15
  261.3 2.6 copy-start.16
  263.8 88.9 %copy-start.6 = (f32[4,1024]{1,0:T(4,128)S(1)}, f32[4,1024]{1,0:T(4,128)}, u32[]{:S(2)}) copy-start(f32[4,1024]{1,0:T(4,128)} %get-tuple-element.952) | copy-start | bytes 49156
  263.9 88.9 %copy-start.7 = (f32[4,1024]{1,0:T(4,128)S(1)}, f32[4,1024]{1,0:T(4,128)}, u32[]{:S(2)}) copy-start(f32[4,1024]{1,0:T(4,128)} %get-tuple-element.953) | copy-start | bytes 49156
  263.9 88.9 %copy-start.8 = (f32[4,1024]{1,0:T(4,128)S(1)}, f32[4,1024]{1,0:T(4,128)}, u32[]{:S(2)}) copy-start(f32[4,1024]{1,0:T(4,128)} %get-tuple-element.954) | copy-start | bytes 49156
  350.6 2.2 copy-start
  350.7 2.9 copy-start.3
  350.7 2.9 copy-start.5
Sparse Core Ops, SparseCore 0:
  9.2 37.4 all-gather.4
  48.5 34.7 all-gather.2
where the time goes:
time: 368 us; the launch traced here: 365 us
  matrix products  110 us (30%)
  waiting for transfers between devices  67.1 us (18%)
  blocking collectives  60.8 us (17%)
  local copies, waits for them, and re-layouts  53.5 us (15%)
  other arithmetic  37 us (10%)
  starting transfers between devices  16.6 us (5%)
  between operations  13.7 us (4%)
  loops' own time  6.32 us (2%)
    all_gather x1, blocking collectives, local(): shard_rows = lax.all_gather(compressed, 'ctx', axis=0, tiled=True)  60.8 us
    dot_general x32, matrix products, online_step(): jnp.dot(weights.astype(jnp.bfloat16), block_kv[:, HD:], preferred_element...  55.7 us
    dot_general x32, matrix products, online_step(): jnp.einsum('qd,kd->qk', query_head, block_kv[:, :HD], preferred_element_t...  53.9 us
    all_gather x1, waiting for transfers between devices, local(): lax.all_gather(keys, 'head', axis=0, tiled=True)  35.7 us
    all_gather x1, waiting for transfers between devices, local(): lax.all_gather(values, 'head', axis=0, tiled=True)  30 us
    reduce_sum x32, other arithmetic, online_step(): running_sum = running_sum * shrink + jnp.sum(weights, axis=-1)  24.2 us
    all_to_all x1, starting transfers between devices, local(): lax.all_to_all(outbox, 'ctx', split_axis=0, concat_axis=0, tiled=True)  9.99 us
    dynamic_slice x16, local copies, waits for them, and re-layouts, heads_step(): return lax.map(per_head, (folded[0], folded[1], folded[2], query_heads))  8.75 us
  transfers between devices with their start and end apart: 5, of which 2 were waited for; matrix products, arithmetic and copies ran while one was open for 29% of the time, Pallas kernels for 0%

commit v1 on v0

--- a/solution.py
+++ b/solution.py
@@ -58,7 +58,9 @@
     local_heads = queries.shape[1] // HD
     group_index = head_index * local_heads // (H // G)
     all_keys, all_values = (
-        lax.all_gather(keys, "head", axis=0, tiled=True),
+        jnp.concatenate(
+            lax.all_to_all(jnp.stack([keys] * lax.axis_size("head")), "head", 0, 0), axis=0
+        ),
         lax.all_gather(values, "head", axis=0, tiled=True),
     )
     group_keys = lax.dynamic_slice_in_dim(all_keys, group_index * HD, HD, 1)

time: 368 us -> 335 us (0.910)
  waiting for transfers between devices: 67.1 us -> 26.9 us
  starting transfers between devices: 16.6 us -> 23.4 us
    all_gather x1 -> x0, waiting for transfers between devices: 35.7 us -> none  [local(): lax.all_gather(keys, 'head', axis=0, tiled=True)]
    all_gather x1, waiting for transfers between devices: 30 us -> 17.4 us  [local(): lax.all_gather(values, 'head', axis=0, tiled=True)]
    all_to_all x0 -> x1, waiting for transfers between devices: none -> 8.79 us  [local(): lax.all_to_all(jnp.stack([keys] * lax.axis_size('head')), 'head', 0, 0)]
    all_to_all x0 -> x1, starting transfers between devices: none -> 5.95 us  [local(): lax.all_to_all(jnp.stack([keys] * lax.axis_size('head')), 'head', 0, 0)]
  transfers between devices with their start and end apart: 5 -> 5, of which waited for: 2 -> 2; matrix products, arithmetic and copies ran while one was open for 29% -> 32% of each run, Pallas kernels for 0% -> 0%
where the time goes in v1:
time: 335 us; the launch traced here: 332 us
  matrix products  110 us (33%)
  blocking collectives  60.8 us (18%)
  local copies, waits for them, and re-layouts  53.5 us (16%)
  other arithmetic  37 us (11%)
  waiting for transfers between devices  26.9 us (8%)
  starting transfers between devices  23.4 us (7%)
  between operations  13.7 us (4%)
  loops' own time  6.32 us (2%)
    all_gather x1, blocking collectives, local(): shard_rows = lax.all_gather(compressed, 'ctx', axis=0, tiled=True)  60.8 us
    dot_general x32, matrix products, online_step(): jnp.dot(weights.astype(jnp.bfloat16), block_kv[:, HD:], preferred_element...  55.7 us
    dot_general x32, matrix products, online_step(): jnp.einsum('qd,kd->qk', query_head, block_kv[:, :HD], preferred_element_t...  54 us
    reduce_sum x32, other arithmetic, online_step(): running_sum = running_sum * shrink + jnp.sum(weights, axis=-1)  24.2 us
    all_gather x1, waiting for transfers between devices, local(): lax.all_gather(values, 'head', axis=0, tiled=True)  17.4 us
    all_to_all x1, starting transfers between devices, local(): lax.all_to_all(outbox, 'ctx', split_axis=0, concat_axis=0, tiled=True)  10.8 us
    all_to_all x1, waiting for transfers between devices, local(): lax.all_to_all(jnp.stack([keys] * lax.axis_size('head')), 'head', 0, 0)  8.79 us
    dynamic_slice x16, local copies, waits for them, and re-layouts, heads_step(): return lax.map(per_head, (folded[0], folded[1], folded[2], query_heads))  8.75 us
  transfers between devices with their start and end apart: 5, of which 2 were waited for; matrix products, arithmetic and copies ran while one was open for 32% of the time, Pallas kernels for 0%

profile of v1, /device:TPU:6, one launch (start us, length us, event | category | flops | bytes accessed | tf_op | source)
XLA Modules:
  0.0 331.7 jit_solution(16600755621538105065)
XLA Ops:
  7.3 2.0 stack.2
  9.2 5.9 %all-to-all-start = ((bf16[16,64,512]{2,1,0:T(8,128)(2,1)}), bf16[16,64,512]{2,1,0:T(8,128)(2,1)S(1)}, u32[]{:S(2)}, u32[]{:S(2)}) async-start(bf16[16,64,512]{2,1,0:T(8,128)(2,1)} %stack.2), calls=%async_computation | async-start | bytes 2097152 | tf_op jit(solution)/shard_map/all_to_all | solution.py:62
  22.8 8.8 %all-to-all-done = bf16[16,64,512]{2,1,0:T(8,128)(2,1)S(1)} async-done(((bf16[16,64,512]{2,1,0:T(8,128)(2,1)}), bf16[16,64,512]{2,1,0:T(8,128)(2,1)S(1)}, u32[]{:S(2)}, u32[]{:S(2)}) %all-to-all-start) | async-done | bytes 1048608 | tf_op jit(solution)/shard_map/all_to_all | solution.py:62
  31.7 17.4 %all-gather.2.cloned.1.call-done = bf16[1024,512]{1,0:T(8,128)(2,1)} async-done(((bf16[64,512]{1,0:T(8,128)(2,1)}), bf16[1024,512]{1,0:T(8,128)(2,1)}) %all-gather.2.cloned.1.call-update) | async-done | bytes 1048592 | tf_op jit(solution)/shard_map/all_gather | solution.py:64
  50.6 3.3 %collective-permute-start = (bf16[16,256]{1,0:T(8,128)(2,1)S(1)}, bf16[16,256]{1,0:T(8,128)(2,1)S(1)}, u32[]{:S(2)}, u32[]{:S(2)}) collective-permute-start(bf16[16,256]{1,0:T(8,128)(2,1)S(1)} %fusion.73), channel_id=1, source_target_pairs={{16,0},{32,16},{48,32},{64,48},{80,64},{96,80},{112,96},{128,112},... | collective-permute-start | bytes 24584 | tf_op jit(solution)/shard_map/ppermute | solution.py:21
  55.0 2.1 copy.45
  57.1 10.8 %all-to-all-start.1 = ((bf16[16,2,16384]{2,1,0:T(2,128)(2,1)}), bf16[16,2,16384]{2,1,0:T(2,128)(2,1)}, u32[]{:S(2)}, u32[]{:S(2)}) async-start(bf16[16,2,16384]{2,1,0:T(2,128)(2,1)} %copy.45), calls=%async_computation.1 | async-start | bytes 2097152 | tf_op jit(solution)/shard_map/all_to_all | solution.py:154
  67.9 3.4 %collective-permute-start.1 = (bf16[512,256]{1,0:T(8,128)(2,1)}, bf16[512,256]{1,0:T(8,128)(2,1)}, u32[]{:S(2)}, u32[]{:S(2)}) collective-permute-start(bf16[512,256]{1,0:T(8,128)(2,1)} %fusion.67), channel_id=1, source_target_pairs={{0,16},{16,32},{32,48},{48,64},{64,80},{80,96},{96,112},{112,128},... | collective-permute-start | bytes 786440 | tf_op jit(solution)/shard_map/ppermute | solution.py:21
  71.5 60.8 %all_gather.7 = bf16[1024,256]{1,0:T(8,128)(2,1)S(1)} all-gather(bf16[64,256]{1,0:T(8,128)(2,1)S(1)} %add_convert_fusion), channel_id=1, replica_groups=mesh['ctx'=16,'head'=16] {'ctx'}, dimensions={0}, use_global_device_ids=true | all-gather | bytes 557056 | tf_op jit(solution)/shard_map/all_gather | solution.py:96
  133.8 40.8 %while.135 = (s32[]{:T(128)}, f32[4,1024]{1,0:T(4,128)S(1)}, f32[4,1024]{1,0:T(4,128)S(1)}, f32[4,1024,128]{2,1,0:T(8,128)}, bf16[2,512,256]{2,1,0:T(8,128)(2,1)...) while((s32[]{:T(128)}, f32[4,1024]{1,0:T(4,128)S(1)}, ...), condition=%wide.region_7.8_spmd.clone, body=%wide.region_2.7_spmd.clone.sunk | while | flops 276044288 | bytes 9548170 | solution.py:107
  135.1 19.0 %while.139 = (s32[]{:T(128)}, f32[4,1024]{1,0:T(4,128)S(1)}, f32[4,1024]{1,0:T(4,128)S(1)}, f32[4,1024,128]{2,1,0:T(8,128)}, bf16[4,1024,128]{2,1,0:T(8,128)(2,1...) while((s32[]{:T(128)}, f32[4,1024]{1,0:T(4,128)S(1)}, ...), condition=%wide.region_6.6_spmd.clone.clone, body=%wide.region_3.5_spmd.clone.clone.sunk | while | flops 276041728 | bytes 9017481 | solution.py:46
  155.5 19.0 %while.139 = (s32[]{:T(128)}, f32[4,1024]{1,0:T(4,128)S(1)}, f32[4,1024]{1,0:T(4,128)S(1)}, f32[4,1024,128]{2,1,0:T(8,128)}, bf16[4,1024,128]{2,1,0:T(8,128)(2,1...) while((s32[]{:T(128)}, f32[4,1024]{1,0:T(4,128)S(1)}, ...), condition=%wide.region_6.6_spmd.clone.clone, body=%wide.region_3.5_spmd.clone.clone.sunk | while | flops 276041728 | bytes 9017481 | solution.py:46
  175.6 49.2 %while.133 = (s32[]{:T(128)}, f32[2,4,512,128]{3,2,1,0:T(8,128)}, s32[2]{0:T(128)S(1)}, bf16[4,1024,128]{2,1,0:T(8,128)(2,1)}, bf16[1536,256]{1,0:T(8,128)(2,1)S...) while((s32[]{:T(128)}, f32[2,4,512,128]{3,2,1,0:T(8,128)}, ...), condition=%wide.region_26.27_spmd, body=%wide.region_21.26_spmd.sunk | while | flops 280826368 | bytes 17762856 | solution.py:130
  176.9 1.9 constant_dynamic-slice_fusion.14
  179.7 19.2 %while.138 = (s32[]{:T(128)}, f32[4,512]{1,0:T(4,128)S(1)}, f32[4,512,128]{2,1,0:T(8,128)S(1)}, bf16[4,512,128]{2,1,0:T(8,128)(2,1)}, bf16[1024,256]{1,0:T(8,128...) while((s32[]{:T(128)}, f32[4,512]{1,0:T(4,128)S(1)}, ...), condition=%wide.region_25.25_spmd.clone, body=%wide.region_22.24_spmd.clone.sunk | while | flops 280560128 | bytes 7259265 | solution.py:46
  179.7 1.9 select_reduce_fusion.6
  182.6 1.9 fusion.107
  184.5 1.8 select_reduce_fusion.6
  187.4 1.9 fusion.107
  189.3 1.9 select_reduce_fusion.6
  192.2 1.9 fusion.107
  194.1 1.8 select_reduce_fusion.6
  197.0 1.9 fusion.107
  201.5 1.9 constant_dynamic-slice_fusion.14
  204.3 19.2 %while.138 = (s32[]{:T(128)}, f32[4,512]{1,0:T(4,128)S(1)}, f32[4,512,128]{2,1,0:T(8,128)S(1)}, bf16[4,512,128]{2,1,0:T(8,128)(2,1)}, bf16[1024,256]{1,0:T(8,128...) while((s32[]{:T(128)}, f32[4,512]{1,0:T(4,128)S(1)}, ...), condition=%wide.region_25.25_spmd.clone, body=%wide.region_22.24_spmd.clone.sunk | while | flops 280560128 | bytes 7259265 | solution.py:46
  204.3 1.8 select_reduce_fusion.6
  207.2 1.9 fusion.107
  209.1 1.9 select_reduce_fusion.6
  212.0 1.9 fusion.107
  213.9 1.8 select_reduce_fusion.6
  216.8 1.9 fusion.107
  218.7 1.9 select_reduce_fusion.6
  221.6 1.9 fusion.107
  224.9 3.1 copy.52
  227.9 2.5 reshape.247
  230.5 86.8 %while.137 = (s32[]{:T(128)}, f32[4,4,256]{2,0,1:T(4,128)S(1)}, f32[4,4,256,128]{3,2,0,1:T(8,128)}, bf16[4,4,256,128]{3,2,0,1:T(8,128)(2,1)}, s32[4,16]{1,0:T(4,...) while((s32[]{:T(128)}, f32[4,4,256]{2,0,1:T(4,128)S(1)}, ...), condition=%wide.wide.region_20.21_spmd.clone, body=%wide.wide.region_14.20_spmd.clone.sunk | while | flops 276336640 | bytes 9205774 | solution.py:172
  233.8 17.5 %while.140 = (s32[]{:T(128)}, f32[4,256]{1,0:T(4,128)S(1)}, f32[4,256,128]{2,1,0:T(8,128)S(1)}, bf16[4,256,128]{2,1,0:T(8,128)(2,1)S(1)}, bf16[2048,256]{1,0:T(8...) while((s32[]{:T(128)}, f32[4,256]{1,0:T(4,128)S(1)}, ...), condition=%wide.region_19.19_spmd.clone, body=%wide.region_16.18_spmd.clone.sunk | while | flops 276333312 | bytes 7583865 | solution.py:46
  236.4 1.8 fusion.98
  240.8 1.8 fusion.98
  242.6 1.7 select_reduce_fusion.5
  245.2 1.8 fusion.98
  247.0 1.7 select_reduce_fusion.5
  249.5 1.8 fusion.98
  255.5 17.5 %while.140 = (s32[]{:T(128)}, f32[4,256]{1,0:T(4,128)S(1)}, f32[4,256,128]{2,1,0:T(8,128)S(1)}, bf16[4,256,128]{2,1,0:T(8,128)(2,1)S(1)}, bf16[2048,256]{1,0:T(8...) while((s32[]{:T(128)}, f32[4,256]{1,0:T(4,128)S(1)}, ...), condition=%wide.region_19.19_spmd.clone, body=%wide.region_16.18_spmd.clone.sunk | while | flops 276333312 | bytes 7583865 | solution.py:46
  258.1 1.8 fusion.98
  262.5 1.8 fusion.98
  266.8 1.8 fusion.98
  268.7 1.7 select_reduce_fusion.5
  271.2 1.8 fusion.98
  277.2 17.5 %while.140 = (s32[]{:T(128)}, f32[4,256]{1,0:T(4,128)S(1)}, f32[4,256,128]{2,1,0:T(8,128)S(1)}, bf16[4,256,128]{2,1,0:T(8,128)(2,1)S(1)}, bf16[2048,256]{1,0:T(8...) while((s32[]{:T(128)}, f32[4,256]{1,0:T(4,128)S(1)}, ...), condition=%wide.region_19.19_spmd.clone, body=%wide.region_16.18_spmd.clone.sunk | while | flops 276333312 | bytes 7583865 | solution.py:46
  279.8 1.8 fusion.98
  281.6 1.7 select_reduce_fusion.5
  284.2 1.8 fusion.98
  288.5 1.8 fusion.98
  290.3 1.7 select_reduce_fusion.5
  292.9 1.8 fusion.98
  298.9 17.5 %while.140 = (s32[]{:T(128)}, f32[4,256]{1,0:T(4,128)S(1)}, f32[4,256,128]{2,1,0:T(8,128)S(1)}, bf16[4,256,128]{2,1,0:T(8,128)(2,1)S(1)}, bf16[2048,256]{1,0:T(8...) while((s32[]{:T(128)}, f32[4,256]{1,0:T(4,128)S(1)}, ...), condition=%wide.region_19.19_spmd.clone, body=%wide.region_16.18_spmd.clone.sunk | while | flops 276333312 | bytes 7583865 | solution.py:46
  301.4 1.8 fusion.98
  305.8 1.8 fusion.98
  307.6 1.7 select_reduce_fusion.5
  310.2 1.8 fusion.98
  314.6 1.8 fusion.98
  317.3 2.1 broadcast_divide_fusion
  320.2 2.8 fusion.64
  (349 shorter events, 114.2 us)
Async XLA Ops:
  6.5 8.7 %copy-start.6 = (bf16[1024,512]{1,0:T(8,128)(2,1)S(1)}, bf16[1024,512]{1,0:T(8,128)(2,1)}, u32[]{:S(2)}) copy-start(bf16[1024,512]{1,0:T(8,128)(2,1)} %param.19) | copy-start | bytes 3145732
  6.5 42.5 %all-gather.2.cloned.1.call-start = ((), (), s32[]{:S(2)}) async-start(), calls=%async_computation.2 | async-start | bytes 1114112 | tf_op jit(solution)/shard_map/all_gather | solution.py:64
  9.2 22.4 %all-to-all-start = ((bf16[16,64,512]{2,1,0:T(8,128)(2,1)}), bf16[16,64,512]{2,1,0:T(8,128)(2,1)S(1)}, u32[]{:S(2)}, u32[]{:S(2)}) async-start(bf16[16,64,512]{2,1,0:T(8,128)(2,1)} %stack.2), calls=%async_computation | async-start | bytes 2097152 | tf_op jit(solution)/shard_map/all_to_all | solution.py:62
  15.2 1.9 copy-start.11
  15.2 6.9 %copy-start.10 = (f32[3,4,1024]{2,1,0:T(4,128)S(1)}, f32[3,4,1024]{2,1,0:T(4,128)}, u32[]{:S(2)}) copy-start(f32[3,4,1024]{2,1,0:T(4,128)} %param.24) | copy-start | bytes 147460
  17.2 0.5 copy-start.15
  18.5 31.8 %copy-start.12 = (s32[16,2]{1,0:T(8,128)}, s32[16,2]{1,0:T(8,128)S(1)}, u32[]{:S(2)}) copy-start(s32[16,2]{1,0:T(8,128)S(1)} %copy.48) | copy-start | bytes 388
  50.6 20.6 %collective-permute-start = (bf16[16,256]{1,0:T(8,128)(2,1)S(1)}, bf16[16,256]{1,0:T(8,128)(2,1)S(1)}, u32[]{:S(2)}, u32[]{:S(2)}) collective-permute-start(bf16[16,256]{1,0:T(8,128)(2,1)S(1)} %fusion.73), channel_id=1, source_target_pairs={{16,0},{32,16},{48,32},{64,48},{80,64},{96,80},{112,96},{128,112},... | collective-permute-start | bytes 24584 | tf_op jit(solution)/shard_map/ppermute | solution.py:21
  57.1 170.8 %all-to-all-start.1 = ((bf16[16,2,16384]{2,1,0:T(2,128)(2,1)}), bf16[16,2,16384]{2,1,0:T(2,128)(2,1)}, u32[]{:S(2)}, u32[]{:S(2)}) async-start(bf16[16,2,16384]{2,1,0:T(2,128)(2,1)} %copy.45), calls=%async_computation.1 | async-start | bytes 2097152 | tf_op jit(solution)/shard_map/all_to_all | solution.py:154
  67.9 106.7 %collective-permute-start.1 = (bf16[512,256]{1,0:T(8,128)(2,1)}, bf16[512,256]{1,0:T(8,128)(2,1)}, u32[]{:S(2)}, u32[]{:S(2)}) collective-permute-start(bf16[512,256]{1,0:T(8,128)(2,1)} %fusion.67), channel_id=1, source_target_pairs={{0,16},{16,32},{32,48},{48,64},{64,80},{80,96},{96,112},{112,128},... | collective-permute-start | bytes 786440 | tf_op jit(solution)/shard_map/ppermute | solution.py:21
  174.6 1.1 copy-start.4
  175.6 4.0 %copy-start.1 = (bf16[1536,256]{1,0:T(8,128)(2,1)}, bf16[1536,256]{1,0:T(8,128)(2,1)S(1)}, u32[]{:S(2)}) copy-start(bf16[1536,256]{1,0:T(8,128)(2,1)S(1)} %get-tuple-element.1592) | copy-start | bytes 2359300 | tf_op jit(solution)/shard_map/while
  198.9 1.4 copy-start.2
  200.3 4.0 %copy-start.1 = (bf16[1536,256]{1,0:T(8,128)(2,1)}, bf16[1536,256]{1,0:T(8,128)(2,1)S(1)}, u32[]{:S(2)}) copy-start(bf16[1536,256]{1,0:T(8,128)(2,1)S(1)} %get-tuple-element.1592) | copy-start | bytes 2359300 | tf_op jit(solution)/shard_map/while
  223.5 1.3 copy-start.2
  227.9 2.6 copy-start.13
  227.9 2.6 copy-start.14
  227.9 2.6 copy-start.16
  227.9 2.6 copy-start.17
  230.5 88.9 %copy-start.7 = (f32[4,1024]{1,0:T(4,128)S(1)}, f32[4,1024]{1,0:T(4,128)}, u32[]{:S(2)}) copy-start(f32[4,1024]{1,0:T(4,128)} %get-tuple-element.952) | copy-start | bytes 49156
  230.5 88.9 %copy-start.8 = (f32[4,1024]{1,0:T(4,128)S(1)}, f32[4,1024]{1,0:T(4,128)}, u32[]{:S(2)}) copy-start(f32[4,1024]{1,0:T(4,128)} %get-tuple-element.953) | copy-start | bytes 49156
  230.5 88.9 %copy-start.9 = (f32[4,1024]{1,0:T(4,128)S(1)}, f32[4,1024]{1,0:T(4,128)}, u32[]{:S(2)}) copy-start(f32[4,1024]{1,0:T(4,128)} %get-tuple-element.954) | copy-start | bytes 49156
  317.3 2.2 copy-start
  317.3 2.9 copy-start.3
  317.3 2.9 copy-start.5
Sparse Core Ops, SparseCore 0:
  9.2 39.7 all-gather.1
